TPU v7x, 512 devices: a whole 4x4x16 slice. The times are simulated.
512 devices in a mesh: exp: 32 (over z, core), rep: 16 (over y, x).
Axes of the slice: x: 4, y: 4, z: 16, core: 2. Of those that a mesh axis runs over, the one named last changes fastest.
Arguments:
- tokens: bfloat16 [65536, 1536], P(('exp', 'rep')), may hold values from -6 to 6
- grad_out: bfloat16 [65536, 1536], P(('exp', 'rep')), may hold values from -6 to 6
- expert_ids: int32 [65536, 2], P(('exp', 'rep')), may hold values from 0 to 31, all different within a row; in each aligned block of 128 rows (0 to 127, 128 to 255, ...) at most 10 rows name the same one
- probs: bfloat16 [65536, 2], P(('exp', 'rep')), may hold values from 0.099609375 to 1
- w_gate: bfloat16 [32, 768, 1536], P('exp', 'rep'), may hold values from -0.15625 to 0.15625
- w_up: bfloat16 [32, 768, 1536], P('exp', 'rep'), may hold values from -0.15625 to 0.15625
- w_down: bfloat16 [32, 768, 1536], P('exp', 'rep'), may hold values from -0.21875 to 0.21875
Outputs:
- grad_tokens: bfloat16 [65536, 1536], P(('exp', 'rep'))
- grad_probs: float32 [65536, 2], P(('exp', 'rep'))
- grad_gate: float32 [32, 768, 1536], P('exp', 'rep')
- grad_up: float32 [32, 768, 1536], P('exp', 'rep')
- grad_down: float32 [32, 768, 1536], P('exp', 'rep')
Inputs may be any that keep to these rules, and one draw needn't show every extreme that they name: `expert_ids`: each token names two different experts; among the 128 tokens of one device no expert is named more than 10 times, a bound that some block reaches.
All inputs are finite; a program needn't handle non-finite values.
Results may differ from a plain program's by a relative error of at most 0.007.
Values may be sent and summed in bfloat16 or wider, within the bound.
No kernel may reach another device: no remote copies, remote signals or barrier semaphores. Data moves between devices by JAX's collectives and lax.ppermute only.
A program may use at most 64 MiB of HBM per device.

v0:
```python
import jax
import jax.numpy as jnp
from jax import lax
from jax.sharding import Mesh
from jax.sharding import PartitionSpec as P

LANE = 128


def swap_pair(value):
    return lax.ppermute(value, "rl", [(0, 1), (1, 0)])


def exchange(blocks):
    shape = blocks.shape
    split = blocks.reshape((lax.axis_size("ez"), lax.axis_size("ec")) + shape[1:])
    split = lax.all_to_all(split, "ez", split_axis=0, concat_axis=0, tiled=True)
    split = lax.all_to_all(split, "ec", split_axis=1, concat_axis=1, tiled=True)
    return split.reshape(shape)


def shards(tokens, grad_out, expert_ids, probs, w_gate, w_up, w_down):
    token_count = tokens.shape[0]
    width = tokens.shape[1]
    exp_count = lax.axis_size("ez") * lax.axis_size("ec")
    capacity = 5 * token_count // (2 * exp_count)
    slots = exp_count * capacity
    chosen = expert_ids.reshape(-1)
    onehot = (chosen[:, None] == jnp.arange(exp_count, dtype=jnp.int32)[None, :]).astype(jnp.int32)
    ranks = jnp.sum((jnp.cumsum(onehot, axis=0) - 1) * onehot, axis=1)
    slot_of = chosen * capacity + ranks
    routing = (slot_of[None, :] == jnp.arange(slots, dtype=jnp.int32)[:, None]).astype(jnp.bfloat16)
    token_routing = routing.reshape(slots, token_count, 2).sum(axis=2)
    prob_pairs = probs.reshape(-1, 1)
    slot_tokens = jnp.dot(token_routing, tokens, preferred_element_type=jnp.float32).astype(
        jnp.bfloat16
    )
    slot_grads = jnp.dot(token_routing, grad_out, preferred_element_type=jnp.float32).astype(
        jnp.bfloat16
    )
    slot_probs = jnp.dot(routing, prob_pairs, preferred_element_type=jnp.float32).astype(
        jnp.bfloat16
    )
    prob_block = jnp.concatenate([slot_probs, jnp.zeros((slots, LANE - 1), jnp.bfloat16)], axis=1)
    send_t = jnp.concatenate([slot_tokens, prob_block], axis=1).reshape(exp_count, capacity, -1)
    arrived_t = exchange(send_t).reshape(slots, -1)
    send_g = slot_grads.reshape(exp_count, capacity, -1)
    arrived_g = exchange(send_g).reshape(slots, -1)
    stacked = jnp.concatenate([w_gate, w_up, w_down], axis=0)
    full = lax.all_gather(stacked, "rh", axis=1, tiled=True)
    gate_w = full[0]
    up_w = full[1]
    down_w = full[2]

    def block(arrived_rows, grads):
        rows = arrived_rows[:, :width]
        weight = arrived_rows[:, width : width + 1].astype(jnp.float32)
        gate = jnp.dot(rows, gate_w.T, preferred_element_type=jnp.float32)
        up = jnp.dot(rows, up_w.T, preferred_element_type=jnp.float32)
        sig = jax.nn.sigmoid(gate)
        act = gate * sig
        hidden = act * up
        back = jnp.dot(grads, down_w.T, preferred_element_type=jnp.float32)
        prob_part = jnp.sum(hidden * back, axis=1, keepdims=True)
        d_gate = (weight * back * up * sig * (1.0 + gate * (1.0 - sig))).astype(jnp.bfloat16)
        d_up = (weight * back * act).astype(jnp.bfloat16)
        weighted = (weight * hidden).astype(jnp.bfloat16)
        partial_rows = jnp.dot(d_gate, gate_w, preferred_element_type=jnp.float32) + jnp.dot(
            d_up, up_w, preferred_element_type=jnp.float32
        )
        packed = jnp.concatenate(
            [
                partial_rows.astype(jnp.bfloat16),
                prob_part.astype(jnp.bfloat16),
                jnp.zeros((rows.shape[0], LANE - 1), jnp.bfloat16),
            ],
            axis=1,
        )
        local = jnp.stack(
            [
                jnp.dot(d_gate.T, rows, preferred_element_type=jnp.float32),
                jnp.dot(d_up.T, rows, preferred_element_type=jnp.float32),
                jnp.dot(weighted.T, grads, preferred_element_type=jnp.float32),
            ]
        )
        return (packed, local)

    partner_t = swap_pair(arrived_t)
    partner_g = swap_pair(arrived_g)
    packed_own, local_own = block(arrived_t, arrived_g)
    packed_partner, local_partner = block(partner_t, partner_g)
    received = swap_pair(packed_partner)
    weight_grads = lax.psum_scatter(
        (local_own + local_partner).astype(jnp.bfloat16), "rh", scatter_dimension=1, tiled=True
    ).astype(jnp.float32)
    summed = (packed_own.astype(jnp.float32) + received.astype(jnp.float32)).astype(jnp.bfloat16)
    returned = exchange(summed.reshape(exp_count, capacity, -1)).reshape(slots, -1)
    grad_tokens = jnp.dot(
        token_routing.T, returned[:, :width], preferred_element_type=jnp.float32
    ).astype(jnp.bfloat16)
    grad_probs = jnp.dot(
        routing.T, returned[:, width : width + 1], preferred_element_type=jnp.float32
    ).reshape(token_count, 2)
    return (grad_tokens, grad_probs, weight_grads[0:1], weight_grads[1:2], weight_grads[2:3])


def solution(mesh):
    exp_count = mesh.shape["exp"]
    rep_count = mesh.shape["rep"]
    view = Mesh(
        mesh.devices.reshape(exp_count // 2, 2, rep_count // 2, 2), ("ez", "ec", "rh", "rl")
    )
    rows_spec = P(("ez", "ec", "rh", "rl"), None)
    weight_spec = P(("ez", "ec"), ("rh", "rl"), None)
    in_specs = (rows_spec,) * 4 + (weight_spec,) * 3
    out_specs = (rows_spec, rows_spec, weight_spec, weight_spec, weight_spec)
    return jax.shard_map(shards, mesh=view, in_specs=in_specs, out_specs=out_specs, check_vma=False)
```

profile of v0, /device:TPU:1, one launch (start us, length us, event | category | flops | bytes accessed | tf_op | source)
XLA Modules:
  0.0 312.6 jit_solution(7887945041732350293)
XLA Ops:
  7.2 0.8 copy.63
  9.4 0.8 copy.67
  13.1 1.9 concatenate.22
  15.0 1.8 copy.69
  16.8 15.9 %all-to-all-start = ((bf16[16,2,10,1664]{3,1,2,0:T(2,128)(2,1)}), bf16[16,2,10,1664]{3,1,2,0:T(2,128)(2,1)S(1)}, u32[]{:S(2)}, u32[]{:S(2)}) async-start(bf16[16,2,10,1664]{3,1,2,0:T(2,128)(2,1)} %copy.69), calls=%async_computation | async-start | bytes 2129920 | tf_op jit(solution)/shard_map/all_to_all | solution.py:17
  32.8 0.8 pad_maximum_fusion
  33.7 1.4 convolution_convert_fusion
  35.0 1.4 reshape_reshape.17
  36.4 2.0 copy.72
  38.4 40.0 %all-to-all-done = bf16[16,2,10,1664]{3,1,2,0:T(2,128)(2,1)S(1)} async-done(((bf16[16,2,10,1664]{3,1,2,0:T(2,128)(2,1)}), bf16[16,2,10,1664]{3,1,2,0:T(2,128)(2,1)S(1)}, u32[]{:S(2)}, u32[]{:S(2)}) %all-to-all-start) | async-done | bytes 1064992 | tf_op jit(solution)/shard_map/all_to_all | solution.py:17
  78.4 10.1 %all_to_all.30 = bf16[16,2,10,1664]{3,0,2,1:T(8,128)(2,1)S(1)} all-to-all(bf16[16,2,10,1664]{3,0,2,1:T(8,128)(2,1)S(1)} %copy.70), channel_id=1, replica_groups=mesh['ez'=16,'ec'=2,'rh'=8,'rl'=2] {'ec'}, dimensions={1} | all-to-all | bytes 2129920 | tf_op jit(solution)/shard_map/all_to_all | solution.py:18
  88.5 7.7 %all-to-all-start.2 = ((bf16[16,2,10,1536]{3,1,2,0:T(2,128)(2,1)}), bf16[16,2,10,1536]{3,1,2,0:T(2,128)(2,1)}, u32[]{:S(2)}, u32[]{:S(2)}) async-start(bf16[16,2,10,1536]{3,1,2,0:T(2,128)(2,1)} %copy.72), calls=%async_computation.2 | async-start | bytes 1966080 | tf_op jit(solution)/shard_map/all_to_all | solution.py:17
  97.0 3.1 %collective-permute-start = (bf16[320,1664]{1,0:T(8,128)(2,1)S(1)}, bf16[320,1664]{1,0:T(8,128)(2,1)}, u32[]{:S(2)}, u32[]{:S(2)}) collective-permute-start(bf16[320,1664]{1,0:T(8,128)(2,1)S(1)} %reshape_reshape.16), channel_id=1, source_target_pairs={{0,1},{1,0},{2,3},{3,2},{4,5},{5,4},{6,7},{7,6},{8,9},{9,8},{10,11... | collective-permute-start | bytes 3194888 | tf_op jit(solution)/shard_map/ppermute | solution.py:11
  100.1 39.4 %all-to-all-done.2 = bf16[16,2,10,1536]{3,1,2,0:T(2,128)(2,1)} async-done(((bf16[16,2,10,1536]{3,1,2,0:T(2,128)(2,1)}), bf16[16,2,10,1536]{3,1,2,0:T(2,128)(2,1)}, u32[]{:S(2)}, u32[]{:S(2)}) %all-to-all-start.2) | async-done | bytes 983072 | tf_op jit(solution)/shard_map/all_to_all | solution.py:17
  139.5 1.4 copy.73
  140.9 9.5 %all_to_all.31 = bf16[16,2,10,1536]{3,0,2,1:T(8,128)(2,1)S(1)} all-to-all(bf16[16,2,10,1536]{3,0,2,1:T(8,128)(2,1)S(1)} %copy.73), channel_id=1, replica_groups=mesh['ez'=16,'ec'=2,'rh'=8,'rl'=2] {'ec'}, dimensions={1} | all-to-all | bytes 1966080 | tf_op jit(solution)/shard_map/all_to_all | solution.py:18
  151.0 1.2 reshape_reshape.18
  152.1 3.3 %collective-permute-start.1 = (bf16[320,1536]{1,0:T(8,128)(2,1)}, bf16[320,1536]{1,0:T(8,128)(2,1)S(1)}, u32[]{:S(2)}, u32[]{:S(2)}) collective-permute-start(bf16[320,1536]{1,0:T(8,128)(2,1)} %reshape_reshape.18), channel_id=1, source_target_pairs={{0,1},{1,0},{2,3},{3,2},{4,5},{5,4},{6,7},{7,6},{8,9},{9,8},{10,11... | collective-permute-start | bytes 2949128 | tf_op jit(solution)/shard_map/ppermute | solution.py:11
  155.6 1.0 convert_reduce_fusion
  156.6 2.1 fusion.11
  160.1 0.9 multiply_reduce_fusion.1
  161.1 0.8 convolution_bitcast_fusion.4
  161.9 0.8 convolution_bitcast_fusion.5
  162.7 0.9 convolution_bitcast_fusion.3
  163.6 1.9 fusion.9
  165.5 1.9 fusion.6
  167.4 9.7 %collective-permute-done.1 = bf16[320,1536]{1,0:T(8,128)(2,1)S(1)} collective-permute-done((bf16[320,1536]{1,0:T(8,128)(2,1)}, bf16[320,1536]{1,0:T(8,128)(2,1)S(1)}, u32[]{:S(2)}, u32[]{:S(2)}) %collective-permute-start.1) | collective-permute-done | bytes 983072 | tf_op jit(solution)/shard_map/ppermute | solution.py:11
  177.2 0.9 multiply_reduce_fusion
  178.1 0.9 convolution_bitcast_fusion
  179.0 2.0 convolution_bitcast_fusion.1
  181.1 2.0 convolution_bitcast_fusion.2
  183.1 2.3 fusion
  186.2 1.3 copy-done.3
  187.4 1.6 fusion.8
  189.1 1.7 fusion.2
  191.4 3.1 concatenate.25
  194.5 3.2 %collective-permute-start.2 = (bf16[320,1664]{1,0:T(8,128)(2,1)}, bf16[320,1664]{1,0:T(8,128)(2,1)}, u32[]{:S(2)}, u32[]{:S(2)}) collective-permute-start(bf16[320,1664]{1,0:T(8,128)(2,1)} %concatenate.25), channel_id=1, source_target_pairs={{0,1},{1,0},{2,3},{3,2},{4,5},{5,4},{6,7},{7,6},{8,9},{9,8},{10,11... | collective-permute-start | bytes 3194888 | tf_op jit(solution)/shard_map/ppermute | solution.py:11
  197.7 0.7 convert_element_type.116
  198.5 1.6 fusion.10
  200.1 1.7 fusion.1
  201.8 2.3 concatenate.24
  204.1 25.7 %collective-permute-done.2 = bf16[320,1664]{1,0:T(8,128)(2,1)} collective-permute-done((bf16[320,1664]{1,0:T(8,128)(2,1)}, bf16[320,1664]{1,0:T(8,128)(2,1)}, u32[]{:S(2)}, u32[]{:S(2)}) %collective-permute-start.2) | collective-permute-done | bytes 1064992 | tf_op jit(solution)/shard_map/ppermute | solution.py:11
  229.8 1.5 add_convert_fusion
  231.7 0.8 copy.77
  232.6 60.0 %all_to_all.32 = bf16[16,2,10,1664]{3,1,2,0:T(2,128)(2,1)S(1)} all-to-all(bf16[16,2,10,1664]{3,1,2,0:T(2,128)(2,1)S(1)} %copy.77), channel_id=1, replica_groups=mesh['ez'=16,'ec'=2,'rh'=8,'rl'=2] {'ez'}, dimensions={0} | all-to-all | bytes 2129920 | tf_op jit(solution)/shard_map/all_to_all | solution.py:17
  292.7 8.3 %all_to_all.33 = bf16[16,2,10,1664]{3,0,2,1:T(8,128)(2,1)S(1)} all-to-all(bf16[16,2,10,1664]{3,0,2,1:T(8,128)(2,1)S(1)} %copy.78), channel_id=1, replica_groups=mesh['ez'=16,'ec'=2,'rh'=8,'rl'=2] {'ec'}, dimensions={1} | all-to-all | bytes 2129920 | tf_op jit(solution)/shard_map/all_to_all | solution.py:18
  302.6 1.1 convolution_convert_fusion.2
  303.7 2.0 fusion.39
  (74 shorter events, 10.7 us)
Async XLA Ops:
  7.2 4.4 %copy-start = (bf16[128,1536]{1,0:T(8,128)(2,1)S(1)}, bf16[128,1536]{1,0:T(8,128)(2,1)}, u32[]{:S(2)}) copy-start(bf16[128,1536]{1,0:T(8,128)(2,1)} %param.7) | copy-start | bytes 1179652
  11.1 22.5 %copy-start.5 = (bf16[320,128]{1,0:T(8,128)(2,1)}, bf16[320,128]{1,0:T(8,128)(2,1)S(1)}, u32[]{:S(2)}) copy-start(bf16[320,128]{1,0:T(8,128)(2,1)S(1)} %fusion.31) | copy-start | bytes 245764
  15.0 17.7 %copy-start.14 = (bf16[1,48,1536]{2,1,0:T(8,128)(2,1)S(1)}, bf16[1,48,1536]{2,1,0:T(8,128)(2,1)}, u32[]{:S(2)}) copy-start(bf16[1,48,1536]{2,1,0:T(8,128)(2,1)} %param.13) | copy-start | bytes 442372
  15.0 17.7 %copy-start.15 = (bf16[1,48,1536]{2,1,0:T(8,128)(2,1)S(1)}, bf16[1,48,1536]{2,1,0:T(8,128)(2,1)}, u32[]{:S(2)}) copy-start(bf16[1,48,1536]{2,1,0:T(8,128)(2,1)} %param.12) | copy-start | bytes 442372
  16.8 15.9 %copy-start.16 = (bf16[1,48,1536]{2,1,0:T(8,128)(2,1)S(1)}, bf16[1,48,1536]{2,1,0:T(8,128)(2,1)}, u32[]{:S(2)}) copy-start(bf16[1,48,1536]{2,1,0:T(8,128)(2,1)} %param.11) | copy-start | bytes 442372
  16.8 16.8 %copy-start.13 = (bf16[128,1536]{1,0:T(8,128)(2,1)S(1)}, bf16[128,1536]{1,0:T(8,128)(2,1)}, u32[]{:S(2)}) copy-start(bf16[128,1536]{1,0:T(8,128)(2,1)} %param.8) | copy-start | bytes 1179652
  16.8 61.5 %all-to-all-start = ((bf16[16,2,10,1664]{3,1,2,0:T(2,128)(2,1)}), bf16[16,2,10,1664]{3,1,2,0:T(2,128)(2,1)S(1)}, u32[]{:S(2)}, u32[]{:S(2)}) async-start(bf16[16,2,10,1664]{3,1,2,0:T(2,128)(2,1)} %copy.69), calls=%async_computation | async-start | bytes 2129920 | tf_op jit(solution)/shard_map/all_to_all | solution.py:17
  32.7 123.9 %all-gather.2.cloned.1.call-start = ((), (), s32[]{:S(2)}) async-start(), calls=%async_computation.7 | async-start | bytes 3981312 | tf_op jit(solution)/shard_map/all_gather | solution.py:50
  88.5 51.0 %all-to-all-start.2 = ((bf16[16,2,10,1536]{3,1,2,0:T(2,128)(2,1)}), bf16[16,2,10,1536]{3,1,2,0:T(2,128)(2,1)}, u32[]{:S(2)}, u32[]{:S(2)}) async-start(bf16[16,2,10,1536]{3,1,2,0:T(2,128)(2,1)} %copy.72), calls=%async_computation.2 | async-start | bytes 1966080 | tf_op jit(solution)/shard_map/all_to_all | solution.py:17
  96.3 207.5 %reduce-scatter.2.cloned.1.call-start = ((), (), s32[]{:S(2)}) async-start(), calls=%async_computation.8 | async-start | bytes 3981312 | tf_op jit(solution)/shard_map/reduce_scatter | solution.py:93
  97.0 58.5 %collective-permute-start = (bf16[320,1664]{1,0:T(8,128)(2,1)S(1)}, bf16[320,1664]{1,0:T(8,128)(2,1)}, u32[]{:S(2)}, u32[]{:S(2)}) collective-permute-start(bf16[320,1664]{1,0:T(8,128)(2,1)S(1)} %reshape_reshape.16), channel_id=1, source_target_pairs={{0,1},{1,0},{2,3},{3,2},{4,5},{5,4},{6,7},{7,6},{8,9},{9,8},{10,11... | collective-permute-start | bytes 3194888 | tf_op jit(solution)/shard_map/ppermute | solution.py:11
  152.1 25.0 %collective-permute-start.1 = (bf16[320,1536]{1,0:T(8,128)(2,1)}, bf16[320,1536]{1,0:T(8,128)(2,1)S(1)}, u32[]{:S(2)}, u32[]{:S(2)}) collective-permute-start(bf16[320,1536]{1,0:T(8,128)(2,1)} %reshape_reshape.18), channel_id=1, source_target_pairs={{0,1},{1,0},{2,3},{3,2},{4,5},{5,4},{6,7},{7,6},{8,9},{9,8},{10,11... | collective-permute-start | bytes 2949128 | tf_op jit(solution)/shard_map/ppermute | solution.py:11
  156.6 2.4 copy-start.2
  158.9 1.2 copy-start.4
  161.1 1.6 copy-start.7
  161.1 1.6 copy-start.9
  178.1 0.9 copy-start.10
  178.1 3.0 copy-start.12
  185.4 2.0 copy-start.3
  185.4 3.6 %copy-start.11 = (bf16[320,384]{1,0:T(8,128)(2,1)S(1)}, bf16[320,384]{1,0:T(8,128)(2,1)}, u32[]{:S(2)}) copy-start(bf16[320,384]{1,0:T(8,128)(2,1)} %copy-done.10) | copy-start | bytes 737284
  194.5 5.6 %copy-start.8 = (bf16[320,384]{1,0:T(8,128)(2,1)S(1)}, bf16[320,384]{1,0:T(8,128)(2,1)}, u32[]{:S(2)}) copy-start(bf16[320,384]{1,0:T(8,128)(2,1)} %copy-done.7) | copy-start | bytes 737284
  194.5 35.4 %collective-permute-start.2 = (bf16[320,1664]{1,0:T(8,128)(2,1)}, bf16[320,1664]{1,0:T(8,128)(2,1)}, u32[]{:S(2)}, u32[]{:S(2)}) collective-permute-start(bf16[320,1664]{1,0:T(8,128)(2,1)} %concatenate.25), channel_id=1, source_target_pairs={{0,1},{1,0},{2,3},{3,2},{4,5},{5,4},{6,7},{7,6},{8,9},{9,8},{10,11... | collective-permute-start | bytes 3194888 | tf_op jit(solution)/shard_map/ppermute | solution.py:11
  301.3 1.3 copy-start.6
  301.3 4.4 %copy-start.1 = (bf16[128,1536]{1,0:T(8,128)(2,1)S(1)}, bf16[128,1536]{1,0:T(8,128)(2,1)}, u32[]{:S(2)}) copy-start(bf16[128,1536]{1,0:T(8,128)(2,1)} %param.7) | copy-start | bytes 1179652
Sparse Core Ops, SparseCore 0:
  36.7 86.7 all-gather.1
  185.6 100.5 reduce-scatter.1
where the time goes:
time: 314 us; the launch traced here: 313 us
  waiting for transfers between devices  115 us (37%)
  blocking collectives  87.9 us (28%)
  starting transfers between devices  33.4 us (11%)
  local copies, waits for them, and re-layouts  28.4 us (9%)
  matrix products  26.3 us (8%)
  between operations  14.5 us (5%)
  other arithmetic  7.28 us (2%)
    all_to_all x2, waiting for transfers between devices, exchange(): split = lax.all_to_all(split, 'ez', split_axis=0, concat_axis=0, tiled=True)  79.3 us
    all_to_all x1, blocking collectives, exchange(): split = lax.all_to_all(split, 'ez', split_axis=0, concat_axis=0, tiled=True)  60 us
    ppermute x3, waiting for transfers between devices, swap_pair(): return lax.ppermute(value, 'rl', [(0, 1), (1, 0)])  35.5 us
    all_to_all x3, blocking collectives, exchange(): split = lax.all_to_all(split, 'ec', split_axis=1, concat_axis=1, tiled=True)  27.9 us
    all_to_all x2, starting transfers between devices, exchange(): split = lax.all_to_all(split, 'ez', split_axis=0, concat_axis=0, tiled=True)  23.6 us
    ppermute x3, starting transfers between devices, swap_pair(): return lax.ppermute(value, 'rl', [(0, 1), (1, 0)])  9.67 us
  transfers between devices with their start and end apart: 7, of which 4 were waited for; matrix products, arithmetic and copies ran while one was open for 13% of the time, Pallas kernels for 0%

commit v1 on v0

--- a/solution.py
+++ b/solution.py
@@ -15,7 +15,9 @@
     shape = blocks.shape
     split = blocks.reshape((lax.axis_size("ez"), lax.axis_size("ec")) + shape[1:])
     split = lax.all_to_all(split, "ez", split_axis=0, concat_axis=0, tiled=True)
-    split = lax.all_to_all(split, "ec", split_axis=1, concat_axis=1, tiled=True)
+    split = jnp.concatenate(
+        lax.all_to_all(jnp.stack(jnp.split(split, lax.axis_size("ec"), axis=1)), "ec", 0, 0), axis=1
+    )
     return split.reshape(shape)
 
 

time: 314 us -> 314 us (level)
  waiting for transfers between devices: 115 us -> 111 us
    split x0 -> x3, local copies, waits for them, and re-layouts: none -> 4.39 us  [exchange(): jnp.split(split, lax.axis_size('ec'), axis=1)]
  transfers between devices with their start and end apart: 7 -> 7, of which waited for: 4 -> 4; matrix products, arithmetic and copies ran while one was open for 13% -> 14% of each run, Pallas kernels for 0% -> 0%
where the time goes in v1:
time: 314 us; the launch traced here: 311 us
  waiting for transfers between devices  111 us (35%)
  blocking collectives  88.6 us (28%)
  starting transfers between devices  33.2 us (11%)
  local copies, waits for them, and re-layouts  29.2 us (9%)
  matrix products  27.5 us (9%)
  between operations  14.5 us (5%)
  other arithmetic  7.58 us (2%)
    all_to_all x2, waiting for transfers between devices, exchange(): split = lax.all_to_all(split, 'ez', split_axis=0, concat_axis=0, tiled=True)  76.8 us
    all_to_all x1, blocking collectives, exchange(): split = lax.all_to_all(split, 'ez', split_axis=0, concat_axis=0, tiled=True)  58.3 us
    ppermute x3, waiting for transfers between devices, swap_pair(): return lax.ppermute(value, 'rl', [(0, 1), (1, 0)])  33.7 us
    all_to_all x3, blocking collectives, exchange(): lax.all_to_all(jnp.stack(jnp.split(split, lax.axis_size('ec'), axis=1)),...  30.3 us
    all_to_all x2, starting transfers between devices, exchange(): split = lax.all_to_all(split, 'ez', split_axis=0, concat_axis=0, tiled=True)  23.6 us
    ppermute x3, starting transfers between devices, swap_pair(): return lax.ppermute(value, 'rl', [(0, 1), (1, 0)])  9.54 us
  transfers between devices with their start and end apart: 7, of which 4 were waited for; matrix products, arithmetic and copies ran while one was open for 14% of the time, Pallas kernels for 0%

profile of v1, /device:TPU:1, one launch (start us, length us, event | category | flops | bytes accessed | tf_op | source)
XLA Modules:
  0.0 311.1 jit_solution(1079149411769462813)
XLA Ops:
  7.2 0.8 copy.100
  12.0 1.3 concatenate.19
  13.4 2.4 concatenate.22
  15.7 1.8 copy.106
  17.5 15.9 %all-to-all-start = ((bf16[16,2,10,1664]{3,1,2,0:T(2,128)(2,1)}), bf16[16,2,10,1664]{3,1,2,0:T(2,128)(2,1)S(1)}, u32[]{:S(2)}, u32[]{:S(2)}) async-start(bf16[16,2,10,1664]{3,1,2,0:T(2,128)(2,1)} %copy.106), calls=%async_computation | async-start | bytes 2129920 | tf_op jit(solution)/shard_map/all_to_all | solution.py:17
  33.5 0.8 pad_maximum_fusion.3
  34.4 1.4 convolution_convert_fusion
  35.8 1.4 reshape_reshape.7
  37.2 2.0 copy.110
  39.2 39.9 %all-to-all-done = bf16[16,2,10,1664]{3,1,2,0:T(2,128)(2,1)S(1)} async-done(((bf16[16,2,10,1664]{3,1,2,0:T(2,128)(2,1)}), bf16[16,2,10,1664]{3,1,2,0:T(2,128)(2,1)S(1)}, u32[]{:S(2)}, u32[]{:S(2)}) %all-to-all-start) | async-done | bytes 1064992 | tf_op jit(solution)/shard_map/all_to_all | solution.py:17
  79.0 1.5 fusion.40
  80.8 10.1 %all_to_all.30 = bf16[2,16,1,10,1664]{4,1,3,2,0:T(8,128)(2,1)S(1)} all-to-all(bf16[2,16,1,10,1664]{4,1,3,2,0:T(8,128)(2,1)S(1)} %pad_maximum_fusion), channel_id=1, replica_groups=mesh['ez'=16,'ec'=2,'rh'=8,'rl'=2] {'ec'}, dimensions={0} | all-to-all | bytes 2129920 | tf_op jit(solution)/shard_map/all_to_all | solution.py:19
  90.9 7.7 %all-to-all-start.2 = ((bf16[16,2,10,1536]{3,1,2,0:T(2,128)(2,1)}), bf16[16,2,10,1536]{3,1,2,0:T(2,128)(2,1)S(1)}, u32[]{:S(2)}, u32[]{:S(2)}) async-start(bf16[16,2,10,1536]{3,1,2,0:T(2,128)(2,1)} %copy.110), calls=%async_computation.2 | async-start | bytes 1966080 | tf_op jit(solution)/shard_map/all_to_all | solution.py:17
  98.7 1.5 copy.109
  100.1 1.6 reshape_reshape_reshape.9
  101.8 3.1 %collective-permute-start = (bf16[320,1664]{1,0:T(8,128)(2,1)S(1)}, bf16[320,1664]{1,0:T(8,128)(2,1)}, u32[]{:S(2)}, u32[]{:S(2)}) collective-permute-start(bf16[320,1664]{1,0:T(8,128)(2,1)S(1)} %reshape_reshape_reshape.9), channel_id=1, source_target_pairs={{0,1},{1,0},{2,3},{3,2},{4,5},{5,4},{6,7},{7,6},{8,9},{9,8},{10,11... | collective-permute-start | bytes 3194888 | tf_op jit(solution)/shard_map/ppermute | solution.py:11
  104.9 36.9 %all-to-all-done.2 = bf16[16,2,10,1536]{3,1,2,0:T(2,128)(2,1)S(1)} async-done(((bf16[16,2,10,1536]{3,1,2,0:T(2,128)(2,1)}), bf16[16,2,10,1536]{3,1,2,0:T(2,128)(2,1)S(1)}, u32[]{:S(2)}, u32[]{:S(2)}) %all-to-all-start.2) | async-done | bytes 983072 | tf_op jit(solution)/shard_map/all_to_all | solution.py:17
  141.8 1.4 fusion.41
  143.6 9.5 %all_to_all.31 = bf16[2,16,1,10,1536]{4,1,3,2,0:T(8,128)(2,1)S(1)} all-to-all(bf16[2,16,1,10,1536]{4,1,3,2,0:T(8,128)(2,1)S(1)} %pad_maximum_fusion.2), channel_id=1, replica_groups=mesh['ez'=16,'ec'=2,'rh'=8,'rl'=2] {'ec'}, dimensions={0} | all-to-all | bytes 1966080 | tf_op jit(solution)/shard_map/all_to_all | solution.py:19
  153.6 1.2 reshape_reshape_reshape.10
  154.8 3.3 %collective-permute-start.1 = (bf16[320,1536]{1,0:T(8,128)(2,1)}, bf16[320,1536]{1,0:T(8,128)(2,1)S(1)}, u32[]{:S(2)}, u32[]{:S(2)}) collective-permute-start(bf16[320,1536]{1,0:T(8,128)(2,1)} %reshape_reshape_reshape.10), channel_id=1, source_target_pairs={{0,1},{1,0},{2,3},{3,2},{4,5},{5,4},{6,7},{7,6},{8,9},{9,8},{10,11... | collective-permute-start | bytes 2949128 | tf_op jit(solution)/shard_map/ppermute | solution.py:11
  158.2 1.0 convert_reduce_fusion
  159.3 2.1 fusion.11
  162.8 0.9 multiply_reduce_fusion.1
  165.4 0.9 convolution_bitcast_fusion.3
  166.3 1.9 fusion.9
  168.2 1.9 fusion.6
  170.1 9.8 %collective-permute-done.1 = bf16[320,1536]{1,0:T(8,128)(2,1)S(1)} collective-permute-done((bf16[320,1536]{1,0:T(8,128)(2,1)}, bf16[320,1536]{1,0:T(8,128)(2,1)S(1)}, u32[]{:S(2)}, u32[]{:S(2)}) %collective-permute-start.1) | collective-permute-done | bytes 983072 | tf_op jit(solution)/shard_map/ppermute | solution.py:11
  179.8 0.9 multiply_reduce_fusion
  180.8 0.9 convolution_bitcast_fusion
  181.7 2.0 convolution_bitcast_fusion.1
  183.7 2.0 convolution_bitcast_fusion.2
  185.7 2.3 fusion
  188.1 1.9 fusion.8
  190.0 2.0 fusion.2
  192.1 1.9 concatenate.25
  194.0 3.1 %collective-permute-start.2 = (bf16[320,1664]{1,0:T(8,128)(2,1)}, bf16[320,1664]{1,0:T(8,128)(2,1)}, u32[]{:S(2)}, u32[]{:S(2)}) collective-permute-start(bf16[320,1664]{1,0:T(8,128)(2,1)} %concatenate.25), channel_id=1, source_target_pairs={{0,1},{1,0},{2,3},{3,2},{4,5},{5,4},{6,7},{7,6},{8,9},{9,8},{10,11... | collective-permute-start | bytes 3194888 | tf_op jit(solution)/shard_map/ppermute | solution.py:11
  197.2 1.9 fusion.10
  199.2 2.0 fusion.1
  201.1 1.0 concatenate.24
  202.1 24.0 %collective-permute-done.2 = bf16[320,1664]{1,0:T(8,128)(2,1)} collective-permute-done((bf16[320,1664]{1,0:T(8,128)(2,1)}, bf16[320,1664]{1,0:T(8,128)(2,1)}, u32[]{:S(2)}, u32[]{:S(2)}) %collective-permute-start.2) | collective-permute-done | bytes 1064992 | tf_op jit(solution)/shard_map/ppermute | solution.py:11
  226.1 1.5 add_convert_fusion
  228.0 0.8 copy.116
  228.8 58.3 %all_to_all.32 = bf16[16,2,10,1664]{3,1,2,0:T(2,128)(2,1)S(1)} all-to-all(bf16[16,2,10,1664]{3,1,2,0:T(2,128)(2,1)S(1)} %copy.116), channel_id=1, replica_groups=mesh['ez'=16,'ec'=2,'rh'=8,'rl'=2] {'ez'}, dimensions={0} | all-to-all | bytes 2129920 | tf_op jit(solution)/shard_map/all_to_all | solution.py:17
  287.1 1.5 fusion.39
  288.8 10.8 %all_to_all.33 = bf16[2,16,1,10,1664]{4,1,3,2,0:T(8,128)(2,1)S(1)} all-to-all(bf16[2,16,1,10,1664]{4,1,3,2,0:T(8,128)(2,1)S(1)} %pad_maximum_fusion.1), channel_id=1, replica_groups=mesh['ez'=16,'ec'=2,'rh'=8,'rl'=2] {'ec'}, dimensions={0} | all-to-all | bytes 2129920 | tf_op jit(solution)/shard_map/all_to_all | solution.py:19
  301.1 1.2 convolution_convert_fusion.2
  302.3 2.0 fusion.42
  (63 shorter events, 10.9 us)
Async XLA Ops:
  7.2 4.4 %copy-start = (bf16[128,1536]{1,0:T(8,128)(2,1)S(1)}, bf16[128,1536]{1,0:T(8,128)(2,1)}, u32[]{:S(2)}) copy-start(bf16[128,1536]{1,0:T(8,128)(2,1)} %param.7) | copy-start | bytes 1179652
  17.5 15.9 %copy-start.5 = (bf16[1,48,1536]{2,1,0:T(8,128)(2,1)S(1)}, bf16[1,48,1536]{2,1,0:T(8,128)(2,1)}, u32[]{:S(2)}) copy-start(bf16[1,48,1536]{2,1,0:T(8,128)(2,1)} %param.13) | copy-start | bytes 442372
  17.5 15.9 %copy-start.6 = (bf16[1,48,1536]{2,1,0:T(8,128)(2,1)S(1)}, bf16[1,48,1536]{2,1,0:T(8,128)(2,1)}, u32[]{:S(2)}) copy-start(bf16[1,48,1536]{2,1,0:T(8,128)(2,1)} %param.12) | copy-start | bytes 442372
  17.5 16.0 %copy-start.7 = (bf16[1,48,1536]{2,1,0:T(8,128)(2,1)S(1)}, bf16[1,48,1536]{2,1,0:T(8,128)(2,1)}, u32[]{:S(2)}) copy-start(bf16[1,48,1536]{2,1,0:T(8,128)(2,1)} %param.11) | copy-start | bytes 442372
  17.5 61.5 %all-to-all-start = ((bf16[16,2,10,1664]{3,1,2,0:T(2,128)(2,1)}), bf16[16,2,10,1664]{3,1,2,0:T(2,128)(2,1)S(1)}, u32[]{:S(2)}, u32[]{:S(2)}) async-start(bf16[16,2,10,1664]{3,1,2,0:T(2,128)(2,1)} %copy.106), calls=%async_computation | async-start | bytes 2129920 | tf_op jit(solution)/shard_map/all_to_all | solution.py:17
  33.4 1.0 copy-start.4
  33.4 125.8 %all-gather.2.cloned.1.call-start = ((), (), s32[]{:S(2)}) async-start(), calls=%async_computation.7 | async-start | bytes 3981312 | tf_op jit(solution)/shard_map/all_gather | solution.py:52
  90.9 50.9 %all-to-all-start.2 = ((bf16[16,2,10,1536]{3,1,2,0:T(2,128)(2,1)}), bf16[16,2,10,1536]{3,1,2,0:T(2,128)(2,1)S(1)}, u32[]{:S(2)}, u32[]{:S(2)}) async-start(bf16[16,2,10,1536]{3,1,2,0:T(2,128)(2,1)} %copy.110), calls=%async_computation.2 | async-start | bytes 1966080 | tf_op jit(solution)/shard_map/all_to_all | solution.py:17
  98.6 203.6 %reduce-scatter.2.cloned.1.call-start = ((), (), s32[]{:S(2)}) async-start(), calls=%async_computation.8 | async-start | bytes 3981312 | tf_op jit(solution)/shard_map/reduce_scatter | solution.py:95
  101.8 56.5 %collective-permute-start = (bf16[320,1664]{1,0:T(8,128)(2,1)S(1)}, bf16[320,1664]{1,0:T(8,128)(2,1)}, u32[]{:S(2)}, u32[]{:S(2)}) collective-permute-start(bf16[320,1664]{1,0:T(8,128)(2,1)S(1)} %reshape_reshape_reshape.9), channel_id=1, source_target_pairs={{0,1},{1,0},{2,3},{3,2},{4,5},{5,4},{6,7},{7,6},{8,9},{9,8},{10,11... | collective-permute-start | bytes 3194888 | tf_op jit(solution)/shard_map/ppermute | solution.py:11
  154.8 25.0 %collective-permute-start.1 = (bf16[320,1536]{1,0:T(8,128)(2,1)}, bf16[320,1536]{1,0:T(8,128)(2,1)S(1)}, u32[]{:S(2)}, u32[]{:S(2)}) collective-permute-start(bf16[320,1536]{1,0:T(8,128)(2,1)} %reshape_reshape_reshape.10), channel_id=1, source_target_pairs={{0,1},{1,0},{2,3},{3,2},{4,5},{5,4},{6,7},{7,6},{8,9},{9,8},{10,11... | collective-permute-start | bytes 2949128 | tf_op jit(solution)/shard_map/ppermute | solution.py:11
  159.3 2.4 copy-start.2
  161.6 1.2 copy-start.3
  194.0 32.1 %collective-permute-start.2 = (bf16[320,1664]{1,0:T(8,128)(2,1)}, bf16[320,1664]{1,0:T(8,128)(2,1)}, u32[]{:S(2)}, u32[]{:S(2)}) collective-permute-start(bf16[320,1664]{1,0:T(8,128)(2,1)} %concatenate.25), channel_id=1, source_target_pairs={{0,1},{1,0},{2,3},{3,2},{4,5},{5,4},{6,7},{7,6},{8,9},{9,8},{10,11... | collective-permute-start | bytes 3194888 | tf_op jit(solution)/shard_map/ppermute | solution.py:11
  301.1 3.1 %copy-start.1 = (bf16[128,1536]{1,0:T(8,128)(2,1)S(1)}, bf16[128,1536]{1,0:T(8,128)(2,1)}, u32[]{:S(2)}) copy-start(bf16[128,1536]{1,0:T(8,128)(2,1)} %param.7) | copy-start | bytes 1179652
Sparse Core Ops, SparseCore 0:
  37.4 82.7 all-gather.1
  188.2 97.8 reduce-scatter.1
